TPU v7x, 512 devices: a whole 4x8x8 slice. The times are simulated.
512 devices in a mesh: req: 64 (over z, x, core), tp: 8 (over y).
Axes of the slice: x: 4, y: 8, z: 8, core: 2. Of those that a mesh axis runs over, the one named last changes fastest.
Arguments:
- q_new: bfloat16 [4096, 5120], P('req', 'tp'), may hold values from -6 to 6
- k_new: bfloat16 [4096, 1024], P('req', 'tp'), may hold values from -15 to 15
- v_new: bfloat16 [4096, 1024], P('req', 'tp'), may hold values from -6 to 6
- k_cache: bfloat16 [1024, 128, 1024], P('req', None, 'tp'), may hold values from -16 to 16
- v_cache: bfloat16 [1024, 128, 1024], P('req', None, 'tp'), may hold values from -6 to 6
- lengths: int32 [32], replicated, may hold values from 1 to 4096, as said below
- page_table: int32 [32, 32], replicated, may hold values from -1 to 1023, as said below
- w_out: bfloat16 [5120, 5120], P('req', 'tp'), may hold values from -0.078125 to 0.078125
Outputs:
- attn_out: bfloat16 [4096, 5120], P('req')
Inputs may be any that keep to these rules, and one draw needn't show every extreme that they name: `lengths`: the last request, 31, has exactly 4096 cached tokens; every request has at least one. `page_table`: request r uses ceil(lengths[r] / 128) logical pages. Its first ceil(ceil(lengths[r] / 128) / 2) logical pages lie among global pages 2r * 16 to (2r + 1) * 16 - 1, the rest among (2r + 1) * 16 to (2r + 2) * 16 - 1; distinct logical pages use distinct global pages; entries past a request's last page are -1.
All inputs are finite; a program needn't handle non-finite values.
Results may differ from a plain program's by a relative error of at most 0.024.
Values may be sent and summed in bfloat16 or wider, within the bound.
No kernel may reach another device: no remote copies, remote signals or barrier semaphores. Data moves between devices by JAX's collectives and lax.ppermute only.
A program may use at most 64 MiB of HBM per device.

v0:
```python
import math
import jax
import jax.numpy as jnp
from jax import lax
from jax.sharding import PartitionSpec as P

HD = 128
GROUP = 5
BLOCK_PAGES = 4
ROPE_BASE = 1000000.0
FLOOR_SCORE = -1e30


def from_partner(value, axis, distance):
    return lax.ppermute(value, axis, [(i, i ^ 1 << distance) for i in range(lax.axis_size(axis))])


def from_tp(value, shift):
    if shift == 0:
        return value
    size = lax.axis_size("tp")
    return lax.ppermute(value, "tp", [(i, (i + shift) % size) for i in range(size)])


def rotate(values, places):
    inverse = 1.0 / ROPE_BASE ** (jnp.arange(0, HD, 2).astype(jnp.float32) / HD)
    angles = places.astype(jnp.float32)[:, None] * inverse[None, :]
    cosine = jnp.concatenate([jnp.cos(angles), jnp.cos(angles)], axis=-1)[:, None, :]
    sine = jnp.concatenate([jnp.sin(angles), jnp.sin(angles)], axis=-1)[:, None, :]
    first_half = values[..., : HD // 2]
    second_half = values[..., HD // 2 :]
    turned = jnp.concatenate([-second_half, first_half], axis=-1)
    return values * cosine + turned * sine


def absorb(state, queries, block_keys, block_values, allowed, scale):
    running_max, running_sum, output = state
    scores = (
        jnp.einsum("qcgd,kcd->cgqk", queries, block_keys, preferred_element_type=jnp.float32)
        * scale
    )
    scores = jnp.where(allowed[None, None], scores, FLOOR_SCORE)
    new_max = jnp.maximum(running_max, jnp.max(scores, axis=-1))
    factor = jnp.exp(running_max - new_max)
    weights = jnp.where(allowed[None, None], jnp.exp(scores - new_max[..., None]), 0.0)
    running_sum = running_sum * factor + jnp.sum(weights, axis=-1)
    mixed = jnp.einsum(
        "cgqk,kcd->qcgd",
        weights.astype(jnp.bfloat16),
        block_values,
        preferred_element_type=jnp.float32,
    )
    output = output * jnp.transpose(factor, (2, 0, 1))[..., None] + mixed
    return (new_max, running_sum, output)


def output_rows(w_out):
    parts = lax.axis_size("tp")
    rows, width = w_out.shape
    share = rows // parts
    pieces = lax.all_to_all(w_out.reshape(parts, share, width), "tp", 0, 0, tiled=True)
    mine = jnp.transpose(pieces, (1, 0, 2)).reshape(share, parts * width)
    padded = -(-share // 8) * 8
    mine = jnp.pad(mine, ((0, padded - share), (0, 0)))
    return (lax.all_gather(mine, "req", axis=0, tiled=True), share)


def shards(q_new, k_new, v_new, k_cache, v_cache, lengths, page_table, w_out):
    own_rows = q_new.shape[0]
    all_rows = 2 * own_rows
    local_heads = k_new.shape[1] // HD
    pages_local = k_cache.shape[0]
    page_rows = k_cache.shape[1]
    block_rows = BLOCK_PAGES * page_rows
    scale = 1.0 / math.sqrt(HD)
    weights_mine, share = output_rows(w_out)
    device_row = lax.axis_index("req")
    parity = device_row % 2
    request = device_row // 2
    length = lengths[request]
    own_places = length + parity * own_rows + jnp.arange(own_rows)
    own_queries = rotate(
        q_new.reshape(own_rows, local_heads * GROUP, HD).astype(jnp.float32), own_places
    ).astype(jnp.bfloat16)
    own_keys = rotate(
        k_new.reshape(own_rows, local_heads, HD).astype(jnp.float32), own_places
    ).astype(jnp.bfloat16)
    own_values = v_new.reshape(own_rows, local_heads, HD)
    peer_queries, peer_keys, peer_values = from_partner(
        (own_queries, own_keys, own_values), "req", 0
    )

    def ordered(mine, theirs):
        return jnp.where(
            parity == 0,
            jnp.concatenate([mine, theirs], axis=0),
            jnp.concatenate([theirs, mine], axis=0),
        )

    queries = ordered(own_queries, peer_queries).reshape(all_rows, local_heads, GROUP, HD)
    fresh_keys = ordered(own_keys, peer_keys)
    fresh_values = ordered(own_values, peer_values)
    state = (
        jnp.full((local_heads, GROUP, all_rows), FLOOR_SCORE, jnp.float32),
        jnp.zeros((local_heads, GROUP, all_rows), jnp.float32),
        jnp.zeros((all_rows, local_heads, GROUP, HD), jnp.float32),
    )
    token_index = jnp.arange(all_rows)
    causal = (token_index[None, :] <= token_index[:, None]) & (parity == 1)
    state = absorb(state, queries, fresh_keys, fresh_values, causal, scale)
    page_count = (length + page_rows - 1) // page_rows
    even_pages = (page_count + 1) // 2
    first_page = jnp.where(parity == 0, 0, even_pages)
    last_page = jnp.where(parity == 0, even_pages, page_count)
    table_row = jnp.concatenate([page_table[request], jnp.full((BLOCK_PAGES,), -1, jnp.int32)])
    offset = device_row * pages_local
    block_count = (last_page - first_page + BLOCK_PAGES - 1) // BLOCK_PAGES

    def visit(block, carry):
        block_first = first_page + block * BLOCK_PAGES
        logical = block_first + jnp.arange(BLOCK_PAGES)
        physical = lax.dynamic_slice(table_row, (block_first,), (BLOCK_PAGES,))
        slots = jnp.clip(physical - offset, 0, pages_local - 1)
        block_keys = k_cache[slots].reshape(block_rows, local_heads, HD)
        block_values = v_cache[slots].reshape(block_rows, local_heads, HD)
        key_places = (logical[:, None] * page_rows + jnp.arange(page_rows)[None, :]).reshape(
            block_rows
        )
        usable = jnp.repeat(logical < last_page, page_rows) & (key_places < length)
        allowed = jnp.broadcast_to(usable[None, :], (all_rows, block_rows))
        return absorb(carry, queries, block_keys, block_values, allowed, scale)

    running_max, running_sum, output = lax.fori_loop(0, block_count, visit, state)
    peer_start = (1 - parity) * own_rows
    own_start = parity * own_rows
    outgoing = (
        lax.dynamic_slice_in_dim(output, peer_start, own_rows, 0),
        lax.dynamic_slice_in_dim(running_max, peer_start, own_rows, 2),
        lax.dynamic_slice_in_dim(running_sum, peer_start, own_rows, 2),
    )
    other_output, other_max, other_sum = (
        from_partner(outgoing[0].astype(jnp.bfloat16), "req", 0).astype(jnp.float32),
        from_partner(outgoing[1].astype(jnp.bfloat16), "req", 0).astype(jnp.float32),
        from_partner(outgoing[2].astype(jnp.bfloat16), "req", 0).astype(jnp.float32),
    )
    mine_output = lax.dynamic_slice_in_dim(output, own_start, own_rows, 0)
    mine_max = lax.dynamic_slice_in_dim(running_max, own_start, own_rows, 2)
    mine_sum = lax.dynamic_slice_in_dim(running_sum, own_start, own_rows, 2)
    joint_max = jnp.maximum(mine_max, other_max)
    mine_factor = jnp.exp(mine_max - joint_max)
    other_factor = jnp.exp(other_max - joint_max)
    joint_sum = mine_sum * mine_factor + other_sum * other_factor
    joint_output = (
        mine_output * jnp.transpose(mine_factor, (2, 0, 1))[..., None]
        + other_output * jnp.transpose(other_factor, (2, 0, 1))[..., None]
    )
    attention = (
        (joint_output / jnp.transpose(joint_sum, (2, 0, 1))[..., None])
        .reshape(own_rows, local_heads * GROUP * HD)
        .astype(jnp.bfloat16)
    )
    parts = lax.axis_size("tp")
    full_rows = lax.all_gather(attention, "tp", axis=1, tiled=True)
    projected = lax.dot_general(
        full_rows, weights_mine, (((1,), (1,)), ((), ())), preferred_element_type=jnp.float32
    )
    blocks = weights_mine.shape[0] // (-(-share // 8) * 8)
    projected = projected.reshape(own_rows, blocks, -1)[:, :, :share].astype(jnp.bfloat16)
    gathered = jnp.stack([from_tp(projected, shift) for shift in range(parts)])
    sources = (lax.axis_index("tp") - jnp.arange(parts)) % parts
    gathered = jnp.take(gathered, sources, axis=0)
    return jnp.transpose(gathered, (1, 2, 0, 3)).reshape(own_rows, -1)


def solution(mesh):
    in_specs = (
        P("req", "tp"),
        P("req", "tp"),
        P("req", "tp"),
        P("req", None, "tp"),
        P("req", None, "tp"),
        P(),
        P(),
        P("req", "tp"),
    )
    out_specs = P("req", None)
    return jax.shard_map(shards, mesh=mesh, in_specs=in_specs, out_specs=out_specs, check_vma=False)
```

profile of v0, /device:TPU:9, one launch (start us, length us, event | category | flops | bytes accessed | tf_op | source)
XLA Modules:
  0.0 202.3 jit_solution(11156302024861886297)
XLA Ops:
  6.5 1.0 reshape.364
  7.5 13.9 %all_to_all.5 = bf16[8,10,640]{2,1,0:T(8,128)(2,1)S(1)} all-to-all(bf16[8,10,640]{2,1,0:T(8,128)(2,1)S(1)} %reshape.364), channel_id=1, replica_groups=mesh['req'=64,'tp'=8] {'tp'}, dimensions={0} | all-to-all | bytes 204800 | tf_op jit(solution)/shard_map/all_to_all | solution.py:61
  21.5 0.7 pad.5
  22.2 1.0 reshape.368
  23.2 0.6 dynamic_slice.27
  25.1 4.9 %collective-permute-start.1 = (bf16[64,5,128]{2,1,0:T(8,128)(2,1)S(1)}, bf16[64,5,128]{2,1,0:T(8,128)(2,1)S(1)}, u32[]{:S(2)}, u32[]{:S(2)}) collective-permute-start(bf16[64,5,128]{2,1,0:T(8,128)(2,1)S(1)} %fusion.25), channel_id=1, source_target_pairs={{0,8},{8,0},{16,24},{24,16},{32,40},{40,32},{48,56},{56,48},{64,72... | collective-permute-start | bytes 245768 | tf_op jit(solution)/shard_map/ppermute | solution.py:15
  30.0 1.9 collective-permute-start
  31.9 2.4 %collective-permute-start.2 = (bf16[64,1,128]{2,0,1:T(8,128)(2,1)S(1)}, bf16[64,1,128]{2,0,1:T(8,128)(2,1)S(1)}, u32[]{:S(2)}, u32[]{:S(2)}) collective-permute-start(bf16[64,1,128]{2,0,1:T(8,128)(2,1)S(1)} %bitcast.190), channel_id=1, source_target_pairs={{0,8},{8,0},{16,24},{24,16},{32,40},{40,32},{48,56},{56,48},{64,72... | collective-permute-start | bytes 49160 | tf_op jit(solution)/shard_map/ppermute | solution.py:15
  36.0 20.8 %while.14 = (s32[]{:T(128)}, f32[1,5,128]{2,1,0:T(8,128)S(1)}, f32[1,5,128]{2,1,0:T(8,128)S(1)}, f32[128,1,5,128]{0,3,2,1:T(8,128)S(1)}, s32[]{:T(128)}, /*index...) while((s32[]{:T(128)}, f32[1,5,128]{2,1,0:T(8,128)S(1)}, ...), condition=%wide.region_5.6_spmd, body=%wide.region_2.5_spmd.sunk | while | flops 170889632 | bytes 5585255 | solution.py:133
  36.1 1.6 gather_fusion
  37.8 0.6 fusion.84
  38.4 0.4 bitcast_reduce_fusion.2
  38.8 1.6 gather_fusion.1
  40.4 0.5 fusion.87
  40.9 0.3 fusion.86
  41.3 1.6 gather_fusion
  43.0 0.6 fusion.84
  43.6 0.4 bitcast_reduce_fusion.2
  44.0 1.6 gather_fusion.1
  45.6 0.5 fusion.87
  46.1 0.3 fusion.86
  46.5 1.6 gather_fusion
  48.1 0.6 fusion.84
  48.8 0.4 bitcast_reduce_fusion.2
  49.2 1.6 gather_fusion.1
  50.8 0.5 fusion.87
  51.3 0.3 fusion.86
  51.7 1.6 gather_fusion
  53.3 0.6 fusion.84
  54.0 0.4 bitcast_reduce_fusion.2
  54.3 1.6 gather_fusion.1
  56.0 0.5 fusion.87
  56.5 0.3 fusion.86
  56.8 1.9 collective-permute-start.3
  58.9 2.4 %collective-permute-start.5 = (bf16[1,5,64]{2,1,0:T(8,128)(2,1)S(1)}, bf16[1,5,64]{2,1,0:T(8,128)(2,1)S(1)}, u32[]{:S(2)}, u32[]{:S(2)}) collective-permute-start(bf16[1,5,64]{2,1,0:T(8,128)(2,1)S(1)} %dynamic-slice_convert_fusion.1), channel_id=1, source_target_pairs={{0,8},{8,0},{16,24},{24,16},{32,40},{40,32},{48,56},{56,48},{64,72... | collective-permute-start | bytes 1928 | tf_op jit(solution)/shard_map/ppermute | solution.py:15
  61.4 1.9 collective-permute-start.4
  63.4 1.2 collective-permute-done.4
  64.8 22.3 %all_gather.6 = bf16[64,5120]{0,1:T(8,128)(2,1)S(1)} all-gather(bf16[64,640]{0,1:T(8,128)(2,1)S(1)} %bitcast.187), channel_id=1, replica_groups=mesh['req'=64,'tp'=8] {'tp'}, dimensions={1}, use_global_device_ids=true | all-gather | bytes 737280 | tf_op jit(solution)/shard_map/all_gather | solution.py:163
  87.1 29.9 %all-gather.2.cloned.1.call-done = bf16[1024,5120]{1,0:T(8,128)(2,1)} async-done(((bf16[16,5120]{1,0:T(8,128)(2,1)}), bf16[1024,5120]{1,0:T(8,128)(2,1)}) %all-gather.2.cloned.1.call-update) | async-done | bytes 10485776 | tf_op jit(solution)/shard_map/all_gather | solution.py:65
  117.0 7.3 %convolution_convert_fusion = bf16[64,1024]{1,0:T(8,128)(2,1)S(1)} fusion(bf16[64,5120]{0,1:T(8,128)(2,1)S(1)} %all_gather.6, bf16[1024,5120]{1,0:T(8,128)(2,1)} %all-gather.2.cloned.1.call-done), kind=kOutput, calls=%fused_computation.37 | convolution fusion | flops 671154176 | bytes 11272192 | tf_op jit(solution)/shard_map/dot_general | solution.py:164
  124.5 3.1 %collective-permute-start.6 = (bf16[64,64,10]{0,2,1:T(8,128)(2,1)S(1)}, bf16[64,64,10]{0,2,1:T(8,128)(2,1)S(1)}, u32[]{:S(2)}, u32[]{:S(2)}) collective-permute-start(bf16[64,64,10]{0,2,1:T(8,128)(2,1)S(1)} %bitcast.176), channel_id=1, source_target_pairs={{0,1},{1,2},{2,3},{3,4},{4,5},{5,6},{6,7},{7,0},{8,9},{9,10},{10,1... | collective-permute-start | bytes 245768 | tf_op jit(solution)/shard_map/ppermute | solution.py:22
  127.6 0.7 bitcast_dynamic-update-slice_fusion.7
  128.3 5.2 %collective-permute-start.7 = (bf16[64,64,10]{0,2,1:T(8,128)(2,1)S(1)}, bf16[64,64,10]{0,2,1:T(8,128)(2,1)S(1)}, u32[]{:S(2)}, u32[]{:S(2)}) collective-permute-start(bf16[64,64,10]{0,2,1:T(8,128)(2,1)S(1)} %bitcast.178), channel_id=1, source_target_pairs={{0,2},{1,3},{2,4},{3,5},{4,6},{5,7},{6,0},{7,1},{8,10},{9,11},{10,... | collective-permute-start | bytes 245768 | tf_op jit(solution)/shard_map/ppermute | solution.py:22
  133.6 2.3 %collective-permute-start.8 = (bf16[64,64,10]{0,2,1:T(8,128)(2,1)S(1)}, bf16[64,64,10]{0,2,1:T(8,128)(2,1)S(1)}, u32[]{:S(2)}, u32[]{:S(2)}) collective-permute-start(bf16[64,64,10]{0,2,1:T(8,128)(2,1)S(1)} %bitcast.179), channel_id=1, source_target_pairs={{0,3},{1,4},{2,5},{3,6},{4,7},{5,0},{6,1},{7,2},{8,11},{9,12},{10,... | collective-permute-start | bytes 245768 | tf_op jit(solution)/shard_map/ppermute | solution.py:22
  135.8 4.8 %collective-permute-start.9 = (bf16[64,64,10]{0,2,1:T(8,128)(2,1)S(1)}, bf16[64,64,10]{0,2,1:T(8,128)(2,1)S(1)}, u32[]{:S(2)}, u32[]{:S(2)}) collective-permute-start(bf16[64,64,10]{0,2,1:T(8,128)(2,1)S(1)} %bitcast.180), channel_id=1, source_target_pairs={{0,4},{1,5},{2,6},{3,7},{4,0},{5,1},{6,2},{7,3},{8,12},{9,13},{10,... | collective-permute-start | bytes 245768 | tf_op jit(solution)/shard_map/ppermute | solution.py:22
  140.6 3.3 %collective-permute-start.10 = (bf16[64,64,10]{0,2,1:T(8,128)(2,1)S(1)}, bf16[64,64,10]{0,2,1:T(8,128)(2,1)S(1)}, u32[]{:S(2)}, u32[]{:S(2)}) collective-permute-start(bf16[64,64,10]{0,2,1:T(8,128)(2,1)S(1)} %bitcast.181), channel_id=1, source_target_pairs={{0,5},{1,6},{2,7},{3,0},{4,1},{5,2},{6,3},{7,4},{8,13},{9,14},{10,... | collective-permute-start | bytes 245768 | tf_op jit(solution)/shard_map/ppermute | solution.py:22
  144.0 4.1 %collective-permute-start.11 = (bf16[64,64,10]{0,2,1:T(8,128)(2,1)S(1)}, bf16[64,64,10]{0,2,1:T(8,128)(2,1)S(1)}, u32[]{:S(2)}, u32[]{:S(2)}) collective-permute-start(bf16[64,64,10]{0,2,1:T(8,128)(2,1)S(1)} %bitcast.182), channel_id=1, source_target_pairs={{0,6},{1,7},{2,0},{3,1},{4,2},{5,3},{6,4},{7,5},{8,14},{9,15},{10,... | collective-permute-start | bytes 245768 | tf_op jit(solution)/shard_map/ppermute | solution.py:22
  148.1 0.7 bitcast_dynamic-update-slice_fusion.6
  148.8 4.3 %collective-permute-start.12 = (bf16[64,64,10]{0,2,1:T(8,128)(2,1)S(1)}, bf16[64,64,10]{0,2,1:T(8,128)(2,1)S(1)}, u32[]{:S(2)}, u32[]{:S(2)}) collective-permute-start(bf16[64,64,10]{0,2,1:T(8,128)(2,1)S(1)} %bitcast.183), channel_id=1, source_target_pairs={{0,7},{1,0},{2,1},{3,2},{4,3},{5,4},{6,5},{7,6},{8,15},{9,8},{10,9... | collective-permute-start | bytes 245768 | tf_op jit(solution)/shard_map/ppermute | solution.py:22
  153.1 0.7 bitcast_dynamic-update-slice_fusion.5
  153.8 8.7 %collective-permute-done.8 = bf16[64,64,10]{0,2,1:T(8,128)(2,1)S(1)} collective-permute-done((bf16[64,64,10]{0,2,1:T(8,128)(2,1)S(1)}, bf16[64,64,10]{0,2,1:T(8,128)(2,1)S(1)}, u32[]{:S(2)}, u32[]{:S(2)}) %collective-permute-start.8) | collective-permute-done | bytes 81952 | tf_op jit(solution)/shard_map/ppermute | solution.py:22
  162.6 0.7 bitcast_dynamic-update-slice_fusion.4
  163.3 0.7 bitcast_dynamic-update-slice_fusion.3
  164.0 9.0 %collective-permute-done.10 = bf16[64,64,10]{0,2,1:T(8,128)(2,1)S(1)} collective-permute-done((bf16[64,64,10]{0,2,1:T(8,128)(2,1)S(1)}, bf16[64,64,10]{0,2,1:T(8,128)(2,1)S(1)}, u32[]{:S(2)}, u32[]{:S(2)}) %collective-permute-start.10) | collective-permute-done | bytes 81952 | tf_op jit(solution)/shard_map/ppermute | solution.py:22
  173.0 0.7 bitcast_dynamic-update-slice_fusion.2
  173.8 4.1 %collective-permute-done.11 = bf16[64,64,10]{0,2,1:T(8,128)(2,1)S(1)} collective-permute-done((bf16[64,64,10]{0,2,1:T(8,128)(2,1)S(1)}, bf16[64,64,10]{0,2,1:T(8,128)(2,1)S(1)}, u32[]{:S(2)}, u32[]{:S(2)}) %collective-permute-start.11) | collective-permute-done | bytes 81952 | tf_op jit(solution)/shard_map/ppermute | solution.py:22
  177.9 0.7 bitcast_dynamic-update-slice_fusion.1
  178.6 10.6 %collective-permute-done.12 = bf16[64,64,10]{0,2,1:T(8,128)(2,1)S(1)} collective-permute-done((bf16[64,64,10]{0,2,1:T(8,128)(2,1)S(1)}, bf16[64,64,10]{0,2,1:T(8,128)(2,1)S(1)}, u32[]{:S(2)}, u32[]{:S(2)}) %collective-permute-start.12) | collective-permute-done | bytes 81952 | tf_op jit(solution)/shard_map/ppermute | solution.py:22
  189.2 0.7 bitcast_dynamic-update-slice_fusion
  189.9 2.5 %gather_fusion.2 = bf16[8,64,64,10]{1,3,2,0:T(8,128)(2,1)S(1)} fusion(bf16[8,64,64,10]{1,3,2,0:T(8,128)(2,1)} %bitcast_dynamic-update-slice_fusion, s32[1024]{0:T(1024)S(1)} %pad_clamp_fusion.1), kind=kCustom, calls=%fused_computation.2 | custom fusion | bytes 1310752 | tf_op jit(solution)/shard_map/jit(_take)/gather | solution.py:171
  192.5 0.3 select_bitcast_fusion
  192.7 0.6 copy.22
  193.3 0.8 reshape.367
  194.1 1.3 copy.23
  (77 shorter events, 2.8 us)
Async XLA Ops:
  6.5 28.4 %copy-start = (s32[32,32]{1,0:T(8,128)S(1)}, s32[32,32]{1,0:T(8,128)}, u32[]{:S(2)}) copy-start(s32[32,32]{1,0:T(8,128)} %param.16) | copy-start | bytes 12292
  6.5 16.7 %copy-start.3 = (s32[32]{0:T(128)S(1)}, s32[32]{0:T(128)}, u32[]{:S(2)}) copy-start(s32[32]{0:T(128)} %param.15) | copy-start | bytes 388
  6.5 17.9 %copy-start.1 = (bf16[64,128]{1,0:T(8,128)(2,1)S(1)}, bf16[64,128]{1,0:T(8,128)(2,1)}, u32[]{:S(2)}) copy-start(bf16[64,128]{1,0:T(8,128)(2,1)} %param.11) | copy-start | bytes 49156
  6.5 110.5 %all-gather.2.cloned.1.call-start = ((), (), s32[]{:S(2)}) async-start(), calls=%async_computation.1 | async-start | bytes 10649600 | tf_op jit(solution)/shard_map/all_gather | solution.py:65
  21.4 10.5 %copy-start.2 = (bf16[64,128]{1,0:T(8,128)(2,1)S(1)}, bf16[64,128]{1,0:T(8,128)(2,1)}, u32[]{:S(2)}) copy-start(bf16[64,128]{1,0:T(8,128)(2,1)} %param.12) | copy-start | bytes 49156
  25.1 10.0 %collective-permute-start.1 = (bf16[64,5,128]{2,1,0:T(8,128)(2,1)S(1)}, bf16[64,5,128]{2,1,0:T(8,128)(2,1)S(1)}, u32[]{:S(2)}, u32[]{:S(2)}) collective-permute-start(bf16[64,5,128]{2,1,0:T(8,128)(2,1)S(1)} %fusion.25), channel_id=1, source_target_pairs={{0,8},{8,0},{16,24},{24,16},{32,40},{40,32},{48,56},{56,48},{64,72... | collective-permute-start | bytes 245768 | tf_op jit(solution)/shard_map/ppermute | solution.py:15
  30.0 5.3 %collective-permute-start = (bf16[64,1,128]{2,0,1:T(8,128)(2,1)S(1)}, bf16[64,1,128]{2,0,1:T(8,128)(2,1)S(1)}, u32[]{:S(2)}, u32[]{:S(2)}) collective-permute-start(bf16[64,1,128]{2,0,1:T(8,128)(2,1)S(1)} %bitcast.189), channel_id=1, source_target_pairs={{0,8},{8,0},{16,24},{24,16},{32,40},{40,32},{48,56},{56,48},{64,72... | collective-permute-start | bytes 49160 | tf_op jit(solution)/shard_map/ppermute | solution.py:15
  31.9 3.8 %collective-permute-start.2 = (bf16[64,1,128]{2,0,1:T(8,128)(2,1)S(1)}, bf16[64,1,128]{2,0,1:T(8,128)(2,1)S(1)}, u32[]{:S(2)}, u32[]{:S(2)}) collective-permute-start(bf16[64,1,128]{2,0,1:T(8,128)(2,1)S(1)} %bitcast.190), channel_id=1, source_target_pairs={{0,8},{8,0},{16,24},{24,16},{32,40},{40,32},{48,56},{56,48},{64,72... | collective-permute-start | bytes 49160 | tf_op jit(solution)/shard_map/ppermute | solution.py:15
  56.8 6.5 %collective-permute-start.3 = (bf16[1,5,64]{2,1,0:T(8,128)(2,1)S(1)}, bf16[1,5,64]{2,1,0:T(8,128)(2,1)S(1)}, u32[]{:S(2)}, u32[]{:S(2)}) collective-permute-start(bf16[1,5,64]{2,1,0:T(8,128)(2,1)S(1)} %dynamic-slice_convert_fusion.2), channel_id=1, source_target_pairs={{0,8},{8,0},{16,24},{24,16},{32,40},{40,32},{48,56},{56,48},{64,72... | collective-permute-start | bytes 1928 | tf_op jit(solution)/shard_map/ppermute | solution.py:15
  58.9 4.5 %collective-permute-start.5 = (bf16[1,5,64]{2,1,0:T(8,128)(2,1)S(1)}, bf16[1,5,64]{2,1,0:T(8,128)(2,1)S(1)}, u32[]{:S(2)}, u32[]{:S(2)}) collective-permute-start(bf16[1,5,64]{2,1,0:T(8,128)(2,1)S(1)} %dynamic-slice_convert_fusion.1), channel_id=1, source_target_pairs={{0,8},{8,0},{16,24},{24,16},{32,40},{40,32},{48,56},{56,48},{64,72... | collective-permute-start | bytes 1928 | tf_op jit(solution)/shard_map/ppermute | solution.py:15
  61.4 3.3 %collective-permute-start.4 = (bf16[64,1,5,128]{0,3,2,1:T(8,128)(2,1)S(1)}, bf16[64,1,5,128]{0,3,2,1:T(8,128)(2,1)S(1)}, u32[]{:S(2)}, u32[]{:S(2)}) collective-permute-start(bf16[64,1,5,128]{0,3,2,1:T(8,128)(2,1)S(1)} %dynamic-slice_convert_fusion), channel_id=1, source_target_pairs={{0,8},{8,0},{16,24},{24,16},{32,40},{40,32},{48,56},{56,48},{64,72... | collective-permute-start | bytes 245768 | tf_op jit(solution)/shard_map/ppermute | solution.py:15
  124.5 19.5 %collective-permute-start.6 = (bf16[64,64,10]{0,2,1:T(8,128)(2,1)S(1)}, bf16[64,64,10]{0,2,1:T(8,128)(2,1)S(1)}, u32[]{:S(2)}, u32[]{:S(2)}) collective-permute-start(bf16[64,64,10]{0,2,1:T(8,128)(2,1)S(1)} %bitcast.176), channel_id=1, source_target_pairs={{0,1},{1,2},{2,3},{3,4},{4,5},{5,6},{6,7},{7,0},{8,9},{9,10},{10,1... | collective-permute-start | bytes 245768 | tf_op jit(solution)/shard_map/ppermute | solution.py:22
  128.3 20.5 %collective-permute-start.7 = (bf16[64,64,10]{0,2,1:T(8,128)(2,1)S(1)}, bf16[64,64,10]{0,2,1:T(8,128)(2,1)S(1)}, u32[]{:S(2)}, u32[]{:S(2)}) collective-permute-start(bf16[64,64,10]{0,2,1:T(8,128)(2,1)S(1)} %bitcast.178), channel_id=1, source_target_pairs={{0,2},{1,3},{2,4},{3,5},{4,6},{5,7},{6,0},{7,1},{8,10},{9,11},{10,... | collective-permute-start | bytes 245768 | tf_op jit(solution)/shard_map/ppermute | solution.py:22
  133.6 29.0 %collective-permute-start.8 = (bf16[64,64,10]{0,2,1:T(8,128)(2,1)S(1)}, bf16[64,64,10]{0,2,1:T(8,128)(2,1)S(1)}, u32[]{:S(2)}, u32[]{:S(2)}) collective-permute-start(bf16[64,64,10]{0,2,1:T(8,128)(2,1)S(1)} %bitcast.179), channel_id=1, source_target_pairs={{0,3},{1,4},{2,5},{3,6},{4,7},{5,0},{6,1},{7,2},{8,11},{9,12},{10,... | collective-permute-start | bytes 245768 | tf_op jit(solution)/shard_map/ppermute | solution.py:22
  135.8 27.4 %collective-permute-start.9 = (bf16[64,64,10]{0,2,1:T(8,128)(2,1)S(1)}, bf16[64,64,10]{0,2,1:T(8,128)(2,1)S(1)}, u32[]{:S(2)}, u32[]{:S(2)}) collective-permute-start(bf16[64,64,10]{0,2,1:T(8,128)(2,1)S(1)} %bitcast.180), channel_id=1, source_target_pairs={{0,4},{1,5},{2,6},{3,7},{4,0},{5,1},{6,2},{7,3},{8,12},{9,13},{10,... | collective-permute-start | bytes 245768 | tf_op jit(solution)/shard_map/ppermute | solution.py:22
  140.6 32.4 %collective-permute-start.10 = (bf16[64,64,10]{0,2,1:T(8,128)(2,1)S(1)}, bf16[64,64,10]{0,2,1:T(8,128)(2,1)S(1)}, u32[]{:S(2)}, u32[]{:S(2)}) collective-permute-start(bf16[64,64,10]{0,2,1:T(8,128)(2,1)S(1)} %bitcast.181), channel_id=1, source_target_pairs={{0,5},{1,6},{2,7},{3,0},{4,1},{5,2},{6,3},{7,4},{8,13},{9,14},{10,... | collective-permute-start | bytes 245768 | tf_op jit(solution)/shard_map/ppermute | solution.py:22
  144.0 33.9 %collective-permute-start.11 = (bf16[64,64,10]{0,2,1:T(8,128)(2,1)S(1)}, bf16[64,64,10]{0,2,1:T(8,128)(2,1)S(1)}, u32[]{:S(2)}, u32[]{:S(2)}) collective-permute-start(bf16[64,64,10]{0,2,1:T(8,128)(2,1)S(1)} %bitcast.182), channel_id=1, source_target_pairs={{0,6},{1,7},{2,0},{3,1},{4,2},{5,3},{6,4},{7,5},{8,14},{9,15},{10,... | collective-permute-start | bytes 245768 | tf_op jit(solution)/shard_map/ppermute | solution.py:22
  148.8 40.3 %collective-permute-start.12 = (bf16[64,64,10]{0,2,1:T(8,128)(2,1)S(1)}, bf16[64,64,10]{0,2,1:T(8,128)(2,1)S(1)}, u32[]{:S(2)}, u32[]{:S(2)}) collective-permute-start(bf16[64,64,10]{0,2,1:T(8,128)(2,1)S(1)} %bitcast.183), channel_id=1, source_target_pairs={{0,7},{1,0},{2,1},{3,2},{4,3},{5,4},{6,5},{7,6},{8,15},{9,8},{10,9... | collective-permute-start | bytes 245768 | tf_op jit(solution)/shard_map/ppermute | solution.py:22
Sparse Core Ops, SparseCore 0:
  22.3 94.6 all-gather.1
where the time goes:
time: 203 us; the launch traced here: 202 us
  waiting for transfers between devices  63.6 us (31%)
  starting transfers between devices  42.6 us (21%)
  blocking collectives  36.2 us (18%)
  local copies, waits for them, and re-layouts  27.7 us (14%)
  between operations  15.1 us (7%)
  matrix products  11.1 us (5%)
  other arithmetic  5.6 us (3%)
    ppermute x7, waiting for transfers between devices, from_tp(): lax.ppermute(value, 'tp', [(i, (i + shift) % size) for i in range(size)])  32.5 us
    all_gather x1, waiting for transfers between devices, output_rows(): return (lax.all_gather(mine, 'req', axis=0, tiled=True), share)  29.9 us
    ppermute x7, starting transfers between devices, from_tp(): lax.ppermute(value, 'tp', [(i, (i + shift) % size) for i in range(size)])  27.1 us
    all_gather x1, blocking collectives, shards(): full_rows = lax.all_gather(attention, 'tp', axis=1, tiled=True)  22.3 us
    ppermute x6, starting transfers between devices, from_partner(): lax.ppermute(value, axis, [(i, i ^ 1 << distance) for i in range(lax.axis...  15.4 us
    all_to_all x1, blocking collectives, output_rows(): lax.all_to_all(w_out.reshape(parts, share, width), 'tp', 0, 0, tiled=True)  13.9 us
    dot_general x1, matrix products, shards(): lax.dot_general(full_rows, weights_mine, (((1,), (1,)), ((), ())), prefer...  7.29 us
    gather x4, local copies, waits for them, and re-layouts, visit(): block_values = v_cache[slots].reshape(block_rows, local_heads, HD)  6.49 us
  transfers between devices with their start and end apart: 14, of which 6 were waited for; matrix products, arithmetic and copies ran while one was open for 14% of the time, Pallas kernels for 0%

commit v1 on v0

--- a/solution.py
+++ b/solution.py
@@ -62,7 +62,12 @@
     mine = jnp.transpose(pieces, (1, 0, 2)).reshape(share, parts * width)
     padded = -(-share // 8) * 8
     mine = jnp.pad(mine, ((0, padded - share), (0, 0)))
-    return (lax.all_gather(mine, "req", axis=0, tiled=True), share)
+    return (
+        jnp.concatenate(
+            lax.all_to_all(jnp.stack([mine] * lax.axis_size("req")), "req", 0, 0), axis=0
+        ),
+        share,
+    )
 
 
 def shards(q_new, k_new, v_new, k_cache, v_cache, lengths, page_table, w_out):

time: 203 us -> 338 us (1.67)
  the two profiles are of different devices: /device:TPU:9 before, /device:TPU:69 now
where the time goes in v1:
time: 338 us; the launch traced here: 337 us
  waiting for transfers between devices  198 us (59%)
  starting transfers between devices  51.8 us (15%)
  blocking collectives  36.9 us (11%)
  local copies, waits for them, and re-layouts  23.6 us (7%)
  matrix products  18.8 us (6%)
  other arithmetic  5.81 us (2%)
    all_to_all x1, waiting for transfers between devices, output_rows(): lax.all_to_all(jnp.stack([mine] * lax.axis_size('req')), 'req', 0, 0)  176 us
    ppermute x7, starting transfers between devices, from_tp(): lax.ppermute(value, 'tp', [(i, (i + shift) % size) for i in range(size)])  23.4 us
    all_gather x1, blocking collectives, shards(): full_rows = lax.all_gather(attention, 'tp', axis=1, tiled=True)  22.2 us
    ppermute x7, waiting for transfers between devices, from_tp(): lax.ppermute(value, 'tp', [(i, (i + shift) % size) for i in range(size)])  20.2 us
    dot_general x1, matrix products, shards(): lax.dot_general(full_rows, weights_mine, (((1,), (1,)), ((), ())), prefer...  15.8 us
    all_to_all x1, starting transfers between devices, output_rows(): lax.all_to_all(jnp.stack([mine] * lax.axis_size('req')), 'req', 0, 0)  15.4 us
    all_to_all x1, blocking collectives, output_rows(): lax.all_to_all(w_out.reshape(parts, share, width), 'tp', 0, 0, tiled=True)  14.8 us
    ppermute x6, starting transfers between devices, from_partner(): lax.ppermute(value, axis, [(i, i ^ 1 << distance) for i in range(lax.axis...  13 us
  transfers between devices with their start and end apart: 14, of which 7 were waited for; matrix products, arithmetic and copies ran while one was open for 5% of the time, Pallas kernels for 0%

profile of v1, /device:TPU:69, one launch (start us, length us, event | category | flops | bytes accessed | tf_op | source)
XLA Modules:
  0.0 336.7 jit_solution(9405914986650372419)
XLA Ops:
  0.0 0.9 reshape.366
  1.0 14.8 %all_to_all.10 = bf16[8,10,640]{2,1,0:T(8,128)(2,1)S(1)} all-to-all(bf16[8,10,640]{2,1,0:T(8,128)(2,1)S(1)} %reshape.366), channel_id=1, replica_groups=mesh['req'=64,'tp'=8] {'tp'}, dimensions={0} | all-to-all | bytes 204800 | tf_op jit(solution)/shard_map/all_to_all | solution.py:61
  15.8 5.1 %stack.20 = bf16[64,16,5120]{2,1,0:T(8,128)(2,1)} broadcast(bf16[16,5120]{1,0:T(8,128)(2,1)S(1)} %pad.5), dimensions={1,2} | broadcast | bytes 10649600 | tf_op jit(solution)/shard_map/stack | solution.py:67
  21.0 15.4 %all-to-all-start.1 = ((bf16[64,16,5120]{2,1,0:T(8,128)(2,1)}), bf16[64,16,5120]{2,1,0:T(8,128)(2,1)}, u32[]{:S(2)}, u32[]{:S(2)}) async-start(bf16[64,16,5120]{2,1,0:T(8,128)(2,1)} %stack.20), calls=%async_computation.1 | async-start | bytes 20971520 | tf_op jit(solution)/shard_map/all_to_all | solution.py:67
  36.4 0.1 reshape.369
  36.6 0.6 dynamic_slice.27
  37.9 0.2 multiply_cosine_fusion
  38.2 0.1 fusion.37
  38.3 0.1 slice_negate_fusion
  38.4 0.1 fusion.28
  38.6 2.3 collective-permute-start.1
  40.9 2.1 collective-permute-start
  42.9 2.3 collective-permute-start.2
  46.1 0.1 maximum_select_fusion
  46.2 0.2 fusion.68
  46.5 0.1 maximum_select_fusion.1
  46.7 0.2 fusion.22
  46.9 15.8 %while.14 = (s32[]{:T(128)}, f32[1,5,128]{2,1,0:T(8,128)S(1)}, f32[1,5,128]{2,1,0:T(8,128)S(1)}, f32[128,1,5,128]{0,3,2,1:T(8,128)S(1)}, s32[]{:T(128)}, /*index...) while((s32[]{:T(128)}, f32[1,5,128]{2,1,0:T(8,128)S(1)}, ...), condition=%wide.region_5.6_spmd, body=%wide.region_2.5_spmd.sunk | while | flops 170889632 | bytes 5585263 | solution.py:138
  46.9 0.1 compare_select_fusion.8
  47.0 1.6 gather_fusion
  48.7 0.7 fusion.85
  49.4 0.4 bitcast_reduce_fusion.2
  49.8 0.3 fusion.87
  50.1 1.6 gather_fusion.1
  51.7 0.5 fusion.88
  52.3 1.6 gather_fusion
  53.9 0.7 fusion.85
  54.6 0.4 bitcast_reduce_fusion.2
  55.0 0.3 fusion.87
  55.3 1.6 gather_fusion.1
  56.9 0.5 fusion.88
  57.5 1.6 gather_fusion
  59.2 0.7 fusion.85
  59.9 0.4 bitcast_reduce_fusion.2
  60.3 0.3 fusion.87
  60.6 1.6 gather_fusion.1
  62.2 0.5 fusion.88
  62.8 2.0 collective-permute-start.3
  64.9 2.3 collective-permute-start.5
  67.2 0.1 dynamic-slice_convert_fusion
  67.3 2.1 collective-permute-start.4
  69.4 1.1 collective-permute-done.4
  70.6 0.2 divide_convert_fusion
  70.7 0.1 copy.51
  70.9 22.2 %all_gather.3 = bf16[64,5120]{1,0:T(8,128)(2,1)S(1)} all-gather(bf16[64,640]{1,0:T(8,128)(2,1)S(1)} %copy.51), channel_id=1, replica_groups=mesh['req'=64,'tp'=8] {'tp'}, dimensions={1}, use_global_device_ids=true | all-gather | bytes 737280 | tf_op jit(solution)/shard_map/all_gather | solution.py:168
  93.0 176.2 %all-to-all-done.1 = bf16[64,16,5120]{2,1,0:T(8,128)(2,1)} async-done(((bf16[64,16,5120]{2,1,0:T(8,128)(2,1)}), bf16[64,16,5120]{2,1,0:T(8,128)(2,1)}, u32[]{:S(2)}, u32[]{:S(2)}) %all-to-all-start.1) | async-done | bytes 10485792 | tf_op jit(solution)/shard_map/all_to_all | solution.py:67
  269.3 15.8 %fusion.19 = bf16[64,64,16]{1,0,2:T(8,128)(2,1)S(1)} fusion(bf16[64,16,5120]{2,1,0:T(8,128)(2,1)} %all-to-all-done.1, bf16[64,5120]{1,0:T(8,128)(2,1)S(1)} %all_gather.3), kind=kOutput, calls=%fused_computation.32 | convolution fusion | flops 671088640 | bytes 11272192 | tf_op jit(solution)/shard_map/dot_general | solution.py:169
  285.2 2.4 collective-permute-start.6
  287.6 2.1 collective-permute-start.7
  289.7 3.9 %collective-permute-start.8 = (bf16[64,64,10]{1,0,2:T(8,128)(2,1)S(1)}, bf16[64,64,10]{1,0,2:T(8,128)(2,1)S(1)}, u32[]{:S(2)}, u32[]{:S(2)}) collective-permute-start(bf16[64,64,10]{1,0,2:T(8,128)(2,1)S(1)} %get-tuple-element.146), channel_id=1, source_target_pairs={{0,3},{1,4},{2,5},{3,6},{4,7},{5,0},{6,1},{7,2},{8,11},{9,12},{10,... | collective-permute-start | bytes 245768 | tf_op jit(solution)/shard_map/ppermute | solution.py:22
  293.6 5.1 %collective-permute-start.9 = (bf16[64,64,10]{1,0,2:T(8,128)(2,1)S(1)}, bf16[64,64,10]{1,0,2:T(8,128)(2,1)S(1)}, u32[]{:S(2)}, u32[]{:S(2)}) collective-permute-start(bf16[64,64,10]{1,0,2:T(8,128)(2,1)S(1)} %get-tuple-element.146), channel_id=1, source_target_pairs={{0,4},{1,5},{2,6},{3,7},{4,0},{5,1},{6,2},{7,3},{8,12},{9,13},{10,... | collective-permute-start | bytes 245768 | tf_op jit(solution)/shard_map/ppermute | solution.py:22
  298.7 3.0 collective-permute-start.10
  301.8 4.3 %collective-permute-start.11 = (bf16[64,64,10]{1,0,2:T(8,128)(2,1)S(1)}, bf16[64,64,10]{1,0,2:T(8,128)(2,1)S(1)}, u32[]{:S(2)}, u32[]{:S(2)}) collective-permute-start(bf16[64,64,10]{1,0,2:T(8,128)(2,1)S(1)} %get-tuple-element.146), channel_id=1, source_target_pairs={{0,6},{1,7},{2,0},{3,1},{4,2},{5,3},{6,4},{7,5},{8,14},{9,15},{10,... | collective-permute-start | bytes 245768 | tf_op jit(solution)/shard_map/ppermute | solution.py:22
  306.2 2.5 collective-permute-start.12
  308.7 1.8 collective-permute-done.8
  310.5 3.1 collective-permute-done.9
  313.6 2.0 collective-permute-done.10
  315.7 8.4 %collective-permute-done.11 = bf16[64,64,10]{1,0,2:T(8,128)(2,1)S(1)} collective-permute-done((bf16[64,64,10]{1,0,2:T(8,128)(2,1)S(1)}, bf16[64,64,10]{1,0,2:T(8,128)(2,1)S(1)}, u32[]{:S(2)}, u32[]{:S(2)}) %collective-permute-start.11) | collective-permute-done | bytes 81952 | tf_op jit(solution)/shard_map/ppermute | solution.py:22
  324.1 4.9 %collective-permute-done.12 = bf16[64,64,10]{1,0,2:T(8,128)(2,1)S(1)} collective-permute-done((bf16[64,64,10]{1,0,2:T(8,128)(2,1)S(1)}, bf16[64,64,10]{1,0,2:T(8,128)(2,1)S(1)}, u32[]{:S(2)}, u32[]{:S(2)}) %collective-permute-start.12) | collective-permute-done | bytes 81952 | tf_op jit(solution)/shard_map/ppermute | solution.py:22
  329.0 0.8 gather_fusion.2
  329.8 1.3 select_bitcast_fusion
  331.1 3.5 %copy.43 = bf16[64,64,8,10]{0,3,2,1:T(8,128)(2,1)S(1)} copy(bf16[64,64,8,10]{1,0,3,2:T(8,128)(2,1)} %select_bitcast_fusion) | data formatting | bytes 1310720 | tf_op jit(solution)/shard_map/jit(_take)/select_n | solution.py:176
  334.6 0.8 reshape.368
  335.4 1.3 copy.44
  (66 shorter events, 1.1 us)
Async XLA Ops:
  0.0 45.9 %copy-start = (s32[32,32]{1,0:T(8,128)S(1)}, s32[32,32]{1,0:T(8,128)}, u32[]{:S(2)}) copy-start(s32[32,32]{1,0:T(8,128)} %param.16) | copy-start | bytes 12292
  21.0 15.5 %copy-start.1 = (bf16[64,640]{1,0:T(8,128)(2,1)S(1)}, bf16[64,640]{1,0:T(8,128)(2,1)}, u32[]{:S(2)}) copy-start(bf16[64,640]{1,0:T(8,128)(2,1)} %param.10) | copy-start | bytes 245764
  21.0 15.6 %copy-start.4 = (s32[32]{0:T(128)S(1)}, s32[32]{0:T(128)}, u32[]{:S(2)}) copy-start(s32[32]{0:T(128)} %param.15) | copy-start | bytes 388
  21.0 16.9 %copy-start.2 = (bf16[64,128]{1,0:T(8,128)(2,1)S(1)}, bf16[64,128]{1,0:T(8,128)(2,1)}, u32[]{:S(2)}) copy-start(bf16[64,128]{1,0:T(8,128)(2,1)} %param.11) | copy-start | bytes 49156
  21.0 248.3 %all-to-all-start.1 = ((bf16[64,16,5120]{2,1,0:T(8,128)(2,1)}), bf16[64,16,5120]{2,1,0:T(8,128)(2,1)}, u32[]{:S(2)}, u32[]{:S(2)}) async-start(bf16[64,16,5120]{2,1,0:T(8,128)(2,1)} %stack.20), calls=%async_computation.1 | async-start | bytes 20971520 | tf_op jit(solution)/shard_map/all_to_all | solution.py:67
  36.6 6.4 %copy-start.3 = (bf16[64,128]{1,0:T(8,128)(2,1)S(1)}, bf16[64,128]{1,0:T(8,128)(2,1)}, u32[]{:S(2)}) copy-start(bf16[64,128]{1,0:T(8,128)(2,1)} %param.12) | copy-start | bytes 49156
  38.6 7.5 %collective-permute-start.1 = (bf16[64,5,128]{2,1,0:T(8,128)(2,1)S(1)}, bf16[64,5,128]{2,1,0:T(8,128)(2,1)S(1)}, u32[]{:S(2)}, u32[]{:S(2)}) collective-permute-start(bf16[64,5,128]{2,1,0:T(8,128)(2,1)S(1)} %fusion.28), channel_id=1, source_target_pairs={{0,8},{8,0},{16,24},{24,16},{32,40},{40,32},{48,56},{56,48},{64,72... | collective-permute-start | bytes 245768 | tf_op jit(solution)/shard_map/ppermute | solution.py:15
  40.9 5.3 %collective-permute-start = (bf16[64,1,128]{2,0,1:T(8,128)(2,1)S(1)}, bf16[64,1,128]{2,0,1:T(8,128)(2,1)S(1)}, u32[]{:S(2)}, u32[]{:S(2)}) collective-permute-start(bf16[64,1,128]{2,0,1:T(8,128)(2,1)S(1)} %bitcast.180), channel_id=1, source_target_pairs={{0,8},{8,0},{16,24},{24,16},{32,40},{40,32},{48,56},{56,48},{64,72... | collective-permute-start | bytes 49160 | tf_op jit(solution)/shard_map/ppermute | solution.py:15
  42.9 3.8 %collective-permute-start.2 = (bf16[64,1,128]{2,0,1:T(8,128)(2,1)S(1)}, bf16[64,1,128]{2,0,1:T(8,128)(2,1)S(1)}, u32[]{:S(2)}, u32[]{:S(2)}) collective-permute-start(bf16[64,1,128]{2,0,1:T(8,128)(2,1)S(1)} %bitcast.181), channel_id=1, source_target_pairs={{0,8},{8,0},{16,24},{24,16},{32,40},{40,32},{48,56},{56,48},{64,72... | collective-permute-start | bytes 49160 | tf_op jit(solution)/shard_map/ppermute | solution.py:15
  62.8 6.6 %collective-permute-start.3 = (bf16[1,5,64]{2,1,0:T(8,128)(2,1)S(1)}, bf16[1,5,64]{2,1,0:T(8,128)(2,1)S(1)}, u32[]{:S(2)}, u32[]{:S(2)}) collective-permute-start(bf16[1,5,64]{2,1,0:T(8,128)(2,1)S(1)} %dynamic-slice_convert_fusion.2), channel_id=1, source_target_pairs={{0,8},{8,0},{16,24},{24,16},{32,40},{40,32},{48,56},{56,48},{64,72... | collective-permute-start | bytes 1928 | tf_op jit(solution)/shard_map/ppermute | solution.py:15
  64.9 4.5 %collective-permute-start.5 = (bf16[1,5,64]{2,1,0:T(8,128)(2,1)S(1)}, bf16[1,5,64]{2,1,0:T(8,128)(2,1)S(1)}, u32[]{:S(2)}, u32[]{:S(2)}) collective-permute-start(bf16[1,5,64]{2,1,0:T(8,128)(2,1)S(1)} %dynamic-slice_convert_fusion.1), channel_id=1, source_target_pairs={{0,8},{8,0},{16,24},{24,16},{32,40},{40,32},{48,56},{56,48},{64,72... | collective-permute-start | bytes 1928 | tf_op jit(solution)/shard_map/ppermute | solution.py:15
  67.3 3.3 collective-permute-start.4
  285.2 16.6 %collective-permute-start.6 = (bf16[64,64,10]{1,0,2:T(8,128)(2,1)S(1)}, bf16[64,64,10]{1,0,2:T(8,128)(2,1)S(1)}, u32[]{:S(2)}, u32[]{:S(2)}) collective-permute-start(bf16[64,64,10]{1,0,2:T(8,128)(2,1)S(1)} %get-tuple-element.146), channel_id=1, source_target_pairs={{0,1},{1,2},{2,3},{3,4},{4,5},{5,6},{6,7},{7,0},{8,9},{9,10},{10,1... | collective-permute-start | bytes 245768 | tf_op jit(solution)/shard_map/ppermute | solution.py:22
  287.6 18.6 %collective-permute-start.7 = (bf16[64,64,10]{1,0,2:T(8,128)(2,1)S(1)}, bf16[64,64,10]{1,0,2:T(8,128)(2,1)S(1)}, u32[]{:S(2)}, u32[]{:S(2)}) collective-permute-start(bf16[64,64,10]{1,0,2:T(8,128)(2,1)S(1)} %get-tuple-element.146), channel_id=1, source_target_pairs={{0,2},{1,3},{2,4},{3,5},{4,6},{5,7},{6,0},{7,1},{8,10},{9,11},{10,... | collective-permute-start | bytes 245768 | tf_op jit(solution)/shard_map/ppermute | solution.py:22
  289.7 20.8 %collective-permute-start.8 = (bf16[64,64,10]{1,0,2:T(8,128)(2,1)S(1)}, bf16[64,64,10]{1,0,2:T(8,128)(2,1)S(1)}, u32[]{:S(2)}, u32[]{:S(2)}) collective-permute-start(bf16[64,64,10]{1,0,2:T(8,128)(2,1)S(1)} %get-tuple-element.146), channel_id=1, source_target_pairs={{0,3},{1,4},{2,5},{3,6},{4,7},{5,0},{6,1},{7,2},{8,11},{9,12},{10,... | collective-permute-start | bytes 245768 | tf_op jit(solution)/shard_map/ppermute | solution.py:22
  293.6 20.0 %collective-permute-start.9 = (bf16[64,64,10]{1,0,2:T(8,128)(2,1)S(1)}, bf16[64,64,10]{1,0,2:T(8,128)(2,1)S(1)}, u32[]{:S(2)}, u32[]{:S(2)}) collective-permute-start(bf16[64,64,10]{1,0,2:T(8,128)(2,1)S(1)} %get-tuple-element.146), channel_id=1, source_target_pairs={{0,4},{1,5},{2,6},{3,7},{4,0},{5,1},{6,2},{7,3},{8,12},{9,13},{10,... | collective-permute-start | bytes 245768 | tf_op jit(solution)/shard_map/ppermute | solution.py:22
  298.7 16.9 %collective-permute-start.10 = (bf16[64,64,10]{1,0,2:T(8,128)(2,1)S(1)}, bf16[64,64,10]{1,0,2:T(8,128)(2,1)S(1)}, u32[]{:S(2)}, u32[]{:S(2)}) collective-permute-start(bf16[64,64,10]{1,0,2:T(8,128)(2,1)S(1)} %get-tuple-element.146), channel_id=1, source_target_pairs={{0,5},{1,6},{2,7},{3,0},{4,1},{5,2},{6,3},{7,4},{8,13},{9,14},{10,... | collective-permute-start | bytes 245768 | tf_op jit(solution)/shard_map/ppermute | solution.py:22
  301.8 22.3 %collective-permute-start.11 = (bf16[64,64,10]{1,0,2:T(8,128)(2,1)S(1)}, bf16[64,64,10]{1,0,2:T(8,128)(2,1)S(1)}, u32[]{:S(2)}, u32[]{:S(2)}) collective-permute-start(bf16[64,64,10]{1,0,2:T(8,128)(2,1)S(1)} %get-tuple-element.146), channel_id=1, source_target_pairs={{0,6},{1,7},{2,0},{3,1},{4,2},{5,3},{6,4},{7,5},{8,14},{9,15},{10,... | collective-permute-start | bytes 245768 | tf_op jit(solution)/shard_map/ppermute | solution.py:22
  306.2 22.8 %collective-permute-start.12 = (bf16[64,64,10]{1,0,2:T(8,128)(2,1)S(1)}, bf16[64,64,10]{1,0,2:T(8,128)(2,1)S(1)}, u32[]{:S(2)}, u32[]{:S(2)}) collective-permute-start(bf16[64,64,10]{1,0,2:T(8,128)(2,1)S(1)} %get-tuple-element.146), channel_id=1, source_target_pairs={{0,7},{1,0},{2,1},{3,2},{4,3},{5,4},{6,5},{7,6},{8,15},{9,8},{10,9... | collective-permute-start | bytes 245768 | tf_op jit(solution)/shard_map/ppermute | solution.py:22
